TPU v7x, 512 devices: a whole 4x8x8 slice. The times are simulated.
512 devices in a mesh: pool: 64 (over x, z, core), mp: 8 (over y).
Axes of the slice: x: 4, y: 8, z: 8, core: 2. Of those that a mesh axis runs over, the one named last changes fastest.
Arguments:
- residual_in: bfloat16 [16384, 2048], P('pool', 'mp'), may hold values from -6 to 6
- mlp_branch: bfloat16 [16384, 2048], P('pool'), may hold values from -6 to 6
- norm_gain: float32 [2048], replicated, may hold values from 0.5 to 1.5
- norm_bias: float32 [2048], replicated, may hold values from -3 to 3
- w_qkv: bfloat16 [2048, 3, 2048], P('pool', None, 'mp'), may hold values from -0.125 to 0.125
- qkv_bias: float32 [3, 2048], P(None, 'mp'), may hold values from -3 to 3
- cache_pool: bfloat16 [3072, 2, 32, 2048], P('pool', None, None, 'mp'), as said below
- w_dense: bfloat16 [2048, 2048], P('mp', 'pool'), may hold values from -0.125 to 0.125
- dense_bias: float32 [2048], replicated, may hold values from -3 to 3
- next_gain: float32 [2048], replicated, may hold values from 0.5 to 1.5
- next_bias: float32 [2048], replicated, may hold values from -3 to 3
- w_next: bfloat16 [2048, 3, 2048], P('pool', None, 'mp'), may hold values from -0.125 to 0.125
- next_qkv_bias: float32 [3, 2048], P(None, 'mp'), may hold values from -3 to 3
- token_request: int32 [16384], P('pool'), may hold values from 0 to 255, as said below
- cache_len: int32 [256], P('pool'), may hold values from 0 to 1024, as said below
- block_table: int32 [256, 32], P('pool'), may hold values from 0 to 3071, as said below
Outputs:
- hidden_out: bfloat16 [16384, 2048], P('pool', 'mp')
- next_qkv: bfloat16 [16384, 3, 2048], P('pool', None, 'mp')
Inputs may be any that keep to these rules, and one draw needn't show every extreme that they name: `token_request`: the 256 tokens of index i of pool belong to the requests i * 4 to (i+1) * 4 - 1, each request's tokens in one run, in increasing order, each request with at least one token. `cache_len`: 0 for a fresh prompt; some request has exactly 1024. `block_table`: block b is held by index b // 48 of pool; a block may appear in several lists; entries at or past a request's cached blocks are padding. Of the 128 entries of the requests of one index of pool, exactly 2 name blocks held by each index of pool. `cache_pool`: cached keys and values.
All inputs are finite; a program needn't handle non-finite values.
Results may differ from a plain program's by a relative error of at most 0.015.
Values may be sent and summed in bfloat16 or wider, within the bound.
No kernel may reach another device: no remote copies, remote signals or barrier semaphores. Data moves between devices by JAX's collectives and lax.ppermute only.
A program may use at most 128 MiB of HBM per device.

v0:
```python
import jax
import jax.numpy as jnp
from jax import lax
from jax.sharding import PartitionSpec as P

HEAD_DIM = 64
ROT = 32
epsilon = 1e-05


def layer_norm(row_data, gain_vec, bias_vec):
    values = row_data.astype(jnp.float32)
    row_mean = jnp.mean(values, axis=-1, keepdims=True)
    centered = values - row_mean
    spread = jnp.mean(centered * centered, axis=-1, keepdims=True)
    return centered * lax.rsqrt(spread + epsilon) * gain_vec + bias_vec


def rotate(head_rows, positions):
    half_rot = ROT // 2
    inverse = 10000.0 ** (-2.0 * jnp.arange(half_rot, dtype=jnp.float32) / ROT)
    angles = positions.astype(jnp.float32)[:, None] * inverse[None, :]
    cosine = jnp.cos(angles)[:, None, :]
    sine = jnp.sin(angles)[:, None, :]
    lower = head_rows[..., :half_rot]
    upper = head_rows[..., half_rot:ROT]
    return jnp.concatenate(
        [lower * cosine - upper * sine, upper * cosine + lower * sine, head_rows[..., ROT:]],
        axis=-1,
    )


def run_starts(token_request):
    tok_total = token_request.shape[0]
    token_index = jnp.arange(tok_total, dtype=jnp.int32)
    change = jnp.concatenate([jnp.ones((1,), dtype=bool), token_request[1:] != token_request[:-1]])
    return (token_index, lax.cummax(jnp.where(change, token_index, 0), axis=0))


def row_folder(left_rows, running, w_piece):
    columns_part = lax.slice_in_dim(left_rows, 0, w_piece.shape[0], axis=1)
    return running + jnp.dot(
        columns_part, w_piece.reshape(w_piece.shape[0], -1), preferred_element_type=jnp.float32
    )


def local(
    residual_in,
    mlp_branch,
    norm_gain,
    norm_bias,
    w_qkv,
    qkv_bias,
    cache_pool,
    w_dense,
    dense_bias,
    next_gain,
    next_bias,
    w_next,
    next_qkv_bias,
    token_request,
    cache_len,
    block_table,
):
    full_rows = lax.all_gather(residual_in, "mp", axis=1, tiled=True)
    tok_count = full_rows.shape[0]
    col_width = w_qkv.shape[2]
    head_count = col_width // HEAD_DIM
    normed = layer_norm(full_rows, norm_gain, norm_bias).astype(jnp.bfloat16)
    empty_sum = jnp.zeros((tok_count, 3 * col_width), jnp.float32)
    w_rows = w_qkv.shape[0]
    dense_shard = w_dense.reshape(w_rows, -1)
    joined = jnp.concatenate(
        [w_qkv.reshape(w_rows, -1), w_next.reshape(w_rows, -1), dense_shard], axis=1
    )
    gathered = lax.all_gather(joined, "pool", axis=0, tiled=True)
    qkv_cols = 3 * col_width
    w_qkv_full = gathered[:, :qkv_cols]
    w_next_full = gathered[:, qkv_cols : 2 * qkv_cols]
    pool_total = lax.axis_size("pool")
    w_dense_full = (
        gathered[:, 2 * qkv_cols :]
        .reshape((pool_total,) + w_dense.shape)
        .transpose(1, 0, 2)
        .reshape(w_dense.shape[0], -1)
    )
    projected = row_folder(normed, empty_sum, w_qkv_full)
    projected = (projected + qkv_bias.reshape(1, 3 * col_width)).reshape(tok_count, 3, col_width)
    token_index, starts = run_starts(token_request)
    request_count = cache_len.shape[0]
    local_req = token_request - request_count * lax.axis_index("pool")
    request_ids = jnp.arange(request_count, dtype=jnp.int32)
    request_match = local_req[:, None] == request_ids[None, :]
    cached_here = jnp.sum(jnp.where(request_match, cache_len[None, :], 0), axis=1)
    positions = cached_here + token_index - starts
    query = rotate(projected[:, 0].reshape(tok_count, head_count, HEAD_DIM), positions).astype(
        jnp.bfloat16
    )
    key_new = rotate(projected[:, 1].reshape(tok_count, head_count, HEAD_DIM), positions).astype(
        jnp.bfloat16
    )
    value_new = projected[:, 2].reshape(tok_count, head_count, HEAD_DIM).astype(jnp.bfloat16)
    pool_count = lax.axis_size("pool")
    blocks_here = cache_pool.shape[0]
    entries = block_table.reshape(-1)
    holder_order = jnp.argsort(entries // blocks_here, stable=True)
    slot_ids = (entries % blocks_here)[holder_order].reshape(pool_count, -1)
    wanted = lax.all_to_all(slot_ids, "pool", split_axis=0, concat_axis=0, tiled=True)
    packed = cache_pool[wanted.reshape(-1)].reshape((pool_count, -1) + cache_pool.shape[1:])
    arrived = lax.all_to_all(packed, "pool", split_axis=0, concat_axis=0, tiled=True)
    table_blocks = arrived.reshape((-1,) + cache_pool.shape[1:])[jnp.argsort(holder_order)]
    span = block_table.shape[1] * cache_pool.shape[2]
    slot_total = request_count * span
    cached_keys = table_blocks[:, 0].reshape(slot_total, head_count, HEAD_DIM)
    cached_values = table_blocks[:, 1].reshape(slot_total, head_count, HEAD_DIM)
    slot_index = jnp.arange(slot_total, dtype=jnp.int32)
    slot_req = slot_index // span
    slot_len = jnp.repeat(cache_len, span, total_repeat_length=slot_total)
    cache_ok = (slot_req[None, :] == local_req[:, None]) & (slot_index % span < slot_len)[None, :]
    new_ok = (token_request[None, :] == token_request[:, None]) & (
        token_index[None, :] <= token_index[:, None]
    )
    allowed = jnp.concatenate([cache_ok, new_ok], axis=1)
    key_all = jnp.concatenate([cached_keys, key_new], axis=0).transpose(1, 0, 2)
    value_all = jnp.concatenate([cached_values, value_new], axis=0).transpose(1, 0, 2)
    score_scale = HEAD_DIM ** (-0.5)

    def one_head(operands):
        q_head, k_head, v_head = operands
        scores = (
            jnp.einsum("qd,kd->qk", q_head, k_head, preferred_element_type=jnp.float32)
            * score_scale
        )
        scores = jnp.where(allowed, scores, -1e30)
        row_max = jnp.max(scores, axis=1, keepdims=True)
        weights = jnp.exp(scores - row_max)
        probs = (weights / jnp.sum(weights, axis=1, keepdims=True)).astype(jnp.bfloat16)
        return jnp.dot(probs, v_head, preferred_element_type=jnp.float32).astype(jnp.bfloat16)

    mixed = lax.map(one_head, (query.transpose(1, 0, 2), key_all, value_all))
    attended = mixed.transpose(1, 0, 2).reshape(tok_count, col_width)
    partial_out = jnp.dot(attended, w_dense_full, preferred_element_type=jnp.float32)
    mp_index = lax.axis_index("mp")
    dense_total = lax.psum(partial_out.astype(jnp.bfloat16), "mp").astype(jnp.float32)
    whole_hidden = (
        full_rows.astype(jnp.float32) + dense_total + dense_bias + mlp_branch.astype(jnp.float32)
    ).astype(jnp.bfloat16)
    hidden_out = lax.dynamic_slice_in_dim(whole_hidden, mp_index * col_width, col_width, 1)
    normed_next = layer_norm(whole_hidden, next_gain, next_bias).astype(jnp.bfloat16)
    next_raw = row_folder(normed_next, empty_sum, w_next_full)
    next_qkv = (
        (next_raw + next_qkv_bias.reshape(1, 3 * col_width))
        .astype(jnp.bfloat16)
        .reshape(tok_count, 3, col_width)
    )
    return (hidden_out, next_qkv)


def solution(mesh):
    in_specs = (
        P("pool", "mp"),
        P("pool", None),
        P(),
        P(),
        P("pool", None, "mp"),
        P(None, "mp"),
        P("pool", None, None, "mp"),
        P("mp", "pool"),
        P(),
        P(),
        P(),
        P("pool", None, "mp"),
        P(None, "mp"),
        P("pool"),
        P("pool"),
        P("pool", None),
    )
    out_specs = (P("pool", "mp"), P("pool", None, "mp"))
    return jax.shard_map(local, mesh=mesh, in_specs=in_specs, out_specs=out_specs, check_vma=False)
```

profile of v0, /device:TPU:2, one launch (start us, length us, event | category | flops | bytes accessed | tf_op | source)
XLA Modules:
  0.0 356.8 jit_solution(5560518545241421026)
XLA Ops:
  8.0 0.8 copy.79
  8.9 0.8 copy.91
  9.7 0.8 copy.92
  11.2 0.7 broadcast_divide_fusion
  12.8 2.5 sort.34
  15.4 1.2 gather_fusion
  16.8 22.3 %all_to_all.14 = s32[64,1,2]{2,1,0:T(1,128)S(1)} all-to-all(s32[64,1,2]{2,1,0:T(1,128)S(1)} %bitcast.87), channel_id=1, replica_groups=mesh['pool'=64,'mp'=8] {'pool'}, dimensions={0} | all-to-all | bytes 1024 | tf_op jit(solution)/shard_map/all_to_all | solution.py:108
  39.5 0.7 reduce.7
  40.5 2.8 gather_fusion.1
  43.3 6.6 %all-to-all-start.1 = ((bf16[64,2,2,32,256]{4,3,2,1,0:T(8,128)(2,1)}), bf16[64,2,2,32,256]{4,3,2,1,0:T(8,128)(2,1)}, u32[]{:S(2)}, u32[]{:S(2)}) async-start(bf16[64,2,2,32,256]{4,3,2,1,0:T(8,128)(2,1)} %bitcast.74), calls=%async_computation.1 | async-start | bytes 8388608 | tf_op jit(solution)/shard_map/all_to_all | solution.py:110
  50.6 2.6 sort.35
  54.2 2.6 fusion.63
  57.0 0.7 compare_and_fusion
  57.9 1.4 convert_reduce_fusion
  59.3 1.6 fusion.26
  61.0 97.6 %all-to-all-done.1 = bf16[64,2,2,32,256]{4,3,2,1,0:T(8,128)(2,1)} async-done(((bf16[64,2,2,32,256]{4,3,2,1,0:T(8,128)(2,1)}), bf16[64,2,2,32,256]{4,3,2,1,0:T(8,128)(2,1)}, u32[]{:S(2)}, u32[]{:S(2)}) %all-to-all-start.1) | async-done | bytes 4194336 | tf_op jit(solution)/shard_map/all_to_all | solution.py:110
  158.6 5.0 %gather_fusion.2 = bf16[128,2,32,256]{3,2,1,0:T(8,128)(2,1)} fusion(bf16[128,2,32,256]{3,2,1,0:T(8,128)(2,1)} %bitcast.12, s32[1024]{0:T(1024)S(1)} %pad_clamp_fusion), kind=kCustom, calls=%fused_computation.2 | custom fusion | bytes 8389120 | tf_op jit(solution)/shard_map/gather | solution.py:111
  163.6 4.8 %fusion.70 = (bf16[128,1,32,256]{3,2,1,0:T(8,128)(2,1)}, bf16[128,1,32,256]{3,2,1,0:T(8,128)(2,1)}) fusion(bf16[128,2,32,256]{3,2,1,0:T(8,128)(2,1)} %gather_fusion.2), kind=kLoop, calls=%fused_computation.114 | loop fusion | bytes 8388608 | tf_op jit(solution)/shard_map/slice | solution.py:115
  168.3 7.1 %reshape_squeeze.14 = bf16[4096,4,64]{2,1,0:T(4,128)(2,1)} reshape(bf16[128,1,32,256]{3,2,1,0:T(8,128)(2,1)} %get-tuple-element.110) | data formatting | bytes 4194304 | tf_op jit(solution)/shard_map/reshape;squeeze | solution.py:114
  175.4 7.2 %reshape_squeeze.16 = bf16[4096,4,64]{2,1,0:T(4,128)(2,1)} reshape(bf16[128,1,32,256]{3,2,1,0:T(8,128)(2,1)} %get-tuple-element.109) | data formatting | bytes 4194304 | tf_op jit(solution)/shard_map/reshape;squeeze | solution.py:115
  182.6 3.9 %fusion.37 = f32[256,768]{1,0:T(8,128)} fusion(bf16[2048,1792]{1,0:T(8,128)(2,1)} %all-gather.5.cloned.1.call-done, bf16[256,2048]{1,0:T(8,128)(2,1)S(1)} %copy-done.2, f32[2048]{0:T(1024)S(1)} %copy-done.13, f32[2048]{0:T(1024)S(1)} %copy-done.14, f32[256]{0:T(256)S(1)} %add_rsqrt_fusion.1, f32[256]{0:T(256)S(1)} %broadcast_multiply_fusion.1, ...), kind=kOutput, calls=%fused_computation.49 | convolution fusion | flops 808648704 | bytes 5002240 | tf_op jit(solution)/shard_map/dot_general | solution.py:42
  186.5 1.4 copy.80
  188.2 17.7 %maximum_bitcast_fusion = bf16[4,4352,64]{2,0,1:T(4,128)(2,1)S(1)} fusion(bf16[256,4,64]{2,1,0:T(4,128)(2,1)S(1)} %copy.82, bf16[4096,4,64]{2,1,0:T(4,128)(2,1)} %reshape_squeeze.14), kind=kLoop, calls=%fused_computation.20 | loop fusion | flops 1114112 | bytes 4456448 | tf_op jit(solution)/shard_map/transpose | solution.py:124
  205.9 2.7 copy.85
  208.8 17.9 %maximum_bitcast_fusion.1 = bf16[4,4352,64]{2,0,1:T(4,128)(2,1)S(1)} fusion(bf16[256,4,64]{2,1,0:T(4,128)(2,1)S(1)} %copy.83, bf16[4096,4,64]{2,1,0:T(4,128)(2,1)} %reshape_squeeze.16), kind=kLoop, calls=%fused_computation.21 | loop fusion | flops 1114112 | bytes 4456448 | tf_op jit(solution)/shard_map/transpose | solution.py:125
  226.7 2.6 copy.86
  229.4 21.9 %while.11 = (s32[]{:T(128)}, bf16[4,256,64]{1,2,0:T(8,128)(2,1)S(1)}, bf16[4,256,64]{1,2,0:T(8,128)(2,1)S(1)}, bf16[4,4352,64]{2,1,0:T(8,128)(2,1)}, pred[256,43...) while((s32[]{:T(128)}, bf16[4,256,64]{1,2,0:T(8,128)(2,1)S(1)}, ...), condition=%wide.region_10.11_spmd, body=%wide.region_7.10_spmd.sunk | while | flops 294141440 | bytes 16784460 | solution.py:140
  229.4 2.3 fusion.80
  231.7 0.8 fusion.81
  232.4 2.4 fusion.82
  234.8 2.3 fusion.80
  237.2 0.8 fusion.81
  237.9 2.4 fusion.82
  240.3 2.3 fusion.80
  242.6 0.8 fusion.81
  243.4 2.4 fusion.82
  245.8 2.3 fusion.80
  248.1 0.8 fusion.81
  248.9 2.4 fusion.82
  251.2 1.3 slice.115
  252.5 3.4 reshape.322
  255.9 3.5 copy.87
  259.4 1.6 convolution_convert_fusion
  261.0 80.4 %all-reduce.2.cloned.1.call-done = bf16[256,2048]{1,0:T(8,128)(2,1)} async-done(((bf16[256,2048]{1,0:T(8,128)(2,1)}), bf16[256,2048]{1,0:T(8,128)(2,1)}) %all-reduce.2.cloned.1.call-update) | async-done | bytes 1048592 | tf_op jit(solution)/shard_map/psum | solution.py:144
  341.4 2.2 convert_reduce_fusion.1
  344.6 3.0 fusion.43
  347.8 0.9 copy.89
  348.7 1.6 constant_dynamic-slice_fusion
  (92 shorter events, 6.9 us)
Async XLA Ops:
  7.2 33.3 %copy-start = (bf16[48,2,32,256]{3,2,1,0:T(8,128)(2,1)S(1)}, bf16[48,2,32,256]{3,2,1,0:T(8,128)(2,1)}, u32[]{:S(2)}) copy-start(bf16[48,2,32,256]{3,2,1,0:T(8,128)(2,1)} %param.26) | copy-start | bytes 4718596
  7.2 50.7 %all-gather.3.cloned.1.call-start = ((), (), s32[]{:S(2)}) async-start(), calls=%async_computation.2 | async-start | bytes 1179648 | tf_op jit(solution)/shard_map/all_gather | solution.py:65
  7.9 174.6 %all-gather.5.cloned.1.call-start = ((), (), s32[]{:S(2)}) async-start(), calls=%async_computation.3 | async-start | bytes 7454720 | tf_op jit(solution)/shard_map/all_gather | solution.py:76
  43.2 6.7 %copy-start.8 = (f32[3,256]{1,0:T(4,128)S(1)}, f32[3,256]{1,0:T(4,128)}, u32[]{:S(2)}) copy-start(f32[3,256]{1,0:T(4,128)} %param.25) | copy-start | bytes 9220
  43.2 6.8 %copy-start.5 = (s32[256]{0:T(256)S(1)}, s32[256]{0:T(256)}, u32[]{:S(2)}) copy-start(s32[256]{0:T(256)} %param.33) | copy-start | bytes 3076
  43.2 10.1 %copy-start.6 = (s32[4]{0:T(128)S(1)}, s32[4]{0:T(128)}, u32[]{:S(2)}) copy-start(s32[4]{0:T(128)} %param.34) | copy-start | bytes 52
  43.2 11.0 %copy-start.10 = (pred[4096]{0:T(1024)(128)(4,1)S(1)}, pred[4096]{0:T(1024)(128)(4,1)}, u32[]{:S(2)}) copy-start(pred[4096]{0:T(1024)(128)(4,1)} %constant.223) | copy-start | bytes 12292
  43.2 11.0 %copy-start.11 = (pred[4096]{0:T(1024)(128)(4,1)S(1)}, pred[4096]{0:T(1024)(128)(4,1)}, u32[]{:S(2)}) copy-start(pred[4096]{0:T(1024)(128)(4,1)} %constant.224) | copy-start | bytes 12292
  43.2 10.9 %copy-start.12 = (pred[4096]{0:T(1024)(128)(4,1)S(1)}, pred[4096]{0:T(1024)(128)(4,1)}, u32[]{:S(2)}) copy-start(pred[4096]{0:T(1024)(128)(4,1)} %constant.225) | copy-start | bytes 12292
  43.3 115.3 %all-to-all-start.1 = ((bf16[64,2,2,32,256]{4,3,2,1,0:T(8,128)(2,1)}), bf16[64,2,2,32,256]{4,3,2,1,0:T(8,128)(2,1)}, u32[]{:S(2)}, u32[]{:S(2)}) async-start(bf16[64,2,2,32,256]{4,3,2,1,0:T(8,128)(2,1)} %bitcast.74), calls=%async_computation.1 | async-start | bytes 8388608 | tf_op jit(solution)/shard_map/all_to_all | solution.py:110
  49.9 291.5 %all-reduce.2.cloned.1.call-start = ((), (), s32[]{:S(2)}) async-start(), calls=%async_computation.4 | async-start | bytes 2097152 | tf_op jit(solution)/shard_map/psum | solution.py:144
  175.4 7.2 %copy-start.2 = (bf16[256,2048]{1,0:T(8,128)(2,1)S(1)}, bf16[256,2048]{1,0:T(8,128)(2,1)}, u32[]{:S(2)}) copy-start(bf16[256,2048]{1,0:T(8,128)(2,1)} %all-gather.3.cloned.1.call-done) | copy-start | bytes 3145732
  175.4 7.2 %copy-start.13 = (f32[2048]{0:T(1024)S(1)}, f32[2048]{0:T(1024)}, u32[]{:S(2)}) copy-start(f32[2048]{0:T(1024)} %param.23) | copy-start | bytes 24580
  175.4 7.2 %copy-start.14 = (f32[2048]{0:T(1024)S(1)}, f32[2048]{0:T(1024)}, u32[]{:S(2)}) copy-start(f32[2048]{0:T(1024)} %param.22) | copy-start | bytes 24580
  226.7 2.7 copy-start.4
  255.9 5.1 %copy-start.9 = (f32[3,256]{1,0:T(4,128)S(1)}, f32[3,256]{1,0:T(4,128)}, u32[]{:S(2)}) copy-start(f32[3,256]{1,0:T(4,128)} %param.32) | copy-start | bytes 9220
  255.9 85.5 %copy-start.7 = (f32[2048]{0:T(1024)S(1)}, f32[2048]{0:T(1024)}, u32[]{:S(2)}) copy-start(f32[2048]{0:T(1024)} %param.28) | copy-start | bytes 24580
  261.0 83.6 %copy-start.15 = (f32[2048]{0:T(1024)S(1)}, f32[2048]{0:T(1024)}, u32[]{:S(2)}) copy-start(f32[2048]{0:T(1024)} %param.30) | copy-start | bytes 24580
  261.0 83.6 %copy-start.16 = (f32[2048]{0:T(1024)S(1)}, f32[2048]{0:T(1024)}, u32[]{:S(2)}) copy-start(f32[2048]{0:T(1024)} %param.29) | copy-start | bytes 24580
  343.6 1.0 copy-start.3
  344.0 6.3 %copy-start.1 = (bf16[48,2,32,256]{3,2,1,0:T(8,128)(2,1)S(1)}, bf16[48,2,32,256]{3,2,1,0:T(8,128)(2,1)}, u32[]{:S(2)}) copy-start(bf16[48,2,32,256]{3,2,1,0:T(8,128)(2,1)} %param.26) | copy-start | bytes 4718596
Sparse Core Ops, SparseCore 0:
  10.0 46.8 all-gather.2
  60.8 109.1 all-gather.4
  261.1 80.2 all-reduce.1
where the time goes:
time: 358 us; the launch traced here: 357 us
  waiting for transfers between devices  179 us (50%)
  other arithmetic  56.6 us (16%)
  local copies, waits for them, and re-layouts  51 us (14%)
  matrix products  27.3 us (8%)
  blocking collectives  22.3 us (6%)
  between operations  14.1 us (4%)
  starting transfers between devices  6.75 us (2%)
    all_to_all x1, waiting for transfers between devices, local(): lax.all_to_all(packed, 'pool', split_axis=0, concat_axis=0, tiled=True)  97.6 us
    psum x1, waiting for transfers between devices, local(): lax.psum(partial_out.astype(jnp.bfloat16), 'mp').astype(jnp.float32)  80.4 us
    all_to_all x1, blocking collectives, local(): lax.all_to_all(slot_ids, 'pool', split_axis=0, concat_axis=0, tiled=True)  22.3 us
    transpose x1, other arithmetic, local(): jnp.concatenate([cached_values, value_new], axis=0).transpose(1, 0, 2)  17.9 us
    transpose x1, other arithmetic, local(): key_all = jnp.concatenate([cached_keys, key_new], axis=0).transpose(1, 0, 2)  17.7 us
    dot_general x4, matrix products, one_head(): jnp.dot(probs, v_head, preferred_element_type=jnp.float32)  9.41 us
    dot_general x4, matrix products, one_head(): jnp.einsum('qd,kd->qk', q_head, k_head, preferred_element_type=jnp.float32)  9.37 us
  transfers between devices with their start and end apart: 4, of which 2 were waited for; matrix products, arithmetic and copies ran while one was open for 13% of the time, Pallas kernels for 0%

commit v1 on v0

--- a/solution.py
+++ b/solution.py
@@ -141,7 +141,9 @@
     attended = mixed.transpose(1, 0, 2).reshape(tok_count, col_width)
     partial_out = jnp.dot(attended, w_dense_full, preferred_element_type=jnp.float32)
     mp_index = lax.axis_index("mp")
-    dense_total = lax.psum(partial_out.astype(jnp.bfloat16), "mp").astype(jnp.float32)
+    dense_total = jnp.sum(lax.all_gather(partial_out.astype(jnp.bfloat16), "mp"), axis=0).astype(
+        jnp.float32
+    )
     whole_hidden = (
         full_rows.astype(jnp.float32) + dense_total + dense_bias + mlp_branch.astype(jnp.float32)
     ).astype(jnp.bfloat16)

time: 358 us -> 379 us (1.059)
  the two profiles are of different devices: /device:TPU:2 before, /device:TPU:1 now
where the time goes in v1:
time: 379 us; the launch traced here: 378 us
  waiting for transfers between devices  194 us (51%)
  other arithmetic  61.5 us (16%)
  local copies, waits for them, and re-layouts  51 us (13%)
  matrix products  27.2 us (7%)
  blocking collectives  23.9 us (6%)
  between operations  14.2 us (4%)
  starting transfers between devices  5.96 us (2%)
    all_to_all x1, waiting for transfers between devices, local(): lax.all_to_all(packed, 'pool', split_axis=0, concat_axis=0, tiled=True)  99.8 us
    all_gather x1, waiting for transfers between devices, local(): lax.all_gather(partial_out.astype(jnp.bfloat16), 'mp')  93.6 us
    all_to_all x1, blocking collectives, local(): lax.all_to_all(slot_ids, 'pool', split_axis=0, concat_axis=0, tiled=True)  23.9 us
    transpose x1, other arithmetic, local(): jnp.concatenate([cached_values, value_new], axis=0).transpose(1, 0, 2)  17.9 us
    transpose x1, other arithmetic, local(): key_all = jnp.concatenate([cached_keys, key_new], axis=0).transpose(1, 0, 2)  17.7 us
    dot_general x4, matrix products, one_head(): jnp.dot(probs, v_head, preferred_element_type=jnp.float32)  9.41 us
    dot_general x4, matrix products, one_head(): jnp.einsum('qd,kd->qk', q_head, k_head, preferred_element_type=jnp.float32)  9.37 us
  transfers between devices with their start and end apart: 4, of which 2 were waited for; matrix products, arithmetic and copies ran while one was open for 13% of the time, Pallas kernels for 0%

profile of v1, /device:TPU:1, one launch (start us, length us, event | category | flops | bytes accessed | tf_op | source)
XLA Modules:
  0.0 377.9 jit_solution(17704826116964292634)
XLA Ops:
  8.0 0.8 copy.79
  8.9 0.8 copy.91
  9.7 0.8 copy.92
  12.8 2.5 sort.34
  15.4 1.2 gather_fusion
  16.8 23.9 %all_to_all.14 = s32[64,1,2]{2,1,0:T(1,128)S(1)} all-to-all(s32[64,1,2]{2,1,0:T(1,128)S(1)} %bitcast.89), channel_id=1, replica_groups=mesh['pool'=64,'mp'=8] {'pool'}, dimensions={0} | all-to-all | bytes 1024 | tf_op jit(solution)/shard_map/all_to_all | solution.py:108
  41.2 0.7 reduce.8
  42.1 2.8 gather_fusion.1
  44.9 5.8 %all-to-all-start.1 = ((bf16[64,2,2,32,256]{4,3,2,1,0:T(8,128)(2,1)}), bf16[64,2,2,32,256]{4,3,2,1,0:T(8,128)(2,1)}, u32[]{:S(2)}, u32[]{:S(2)}) async-start(bf16[64,2,2,32,256]{4,3,2,1,0:T(8,128)(2,1)} %bitcast.75), calls=%async_computation.1 | async-start | bytes 8388608 | tf_op jit(solution)/shard_map/all_to_all | solution.py:110
  51.4 2.6 sort.35
  55.1 2.6 fusion.63
  57.9 0.7 compare_and_fusion
  58.8 1.4 convert_reduce_fusion
  60.2 1.6 fusion.26
  61.9 99.8 %all-to-all-done.1 = bf16[64,2,2,32,256]{4,3,2,1,0:T(8,128)(2,1)} async-done(((bf16[64,2,2,32,256]{4,3,2,1,0:T(8,128)(2,1)}), bf16[64,2,2,32,256]{4,3,2,1,0:T(8,128)(2,1)}, u32[]{:S(2)}, u32[]{:S(2)}) %all-to-all-start.1) | async-done | bytes 4194336 | tf_op jit(solution)/shard_map/all_to_all | solution.py:110
  161.6 5.0 %gather_fusion.2 = bf16[128,2,32,256]{3,2,1,0:T(8,128)(2,1)} fusion(bf16[128,2,32,256]{3,2,1,0:T(8,128)(2,1)} %bitcast.12, s32[1024]{0:T(1024)S(1)} %pad_clamp_fusion), kind=kCustom, calls=%fused_computation.2 | custom fusion | bytes 8389120 | tf_op jit(solution)/shard_map/gather | solution.py:111
  166.6 4.7 %fusion.70 = (bf16[128,1,32,256]{3,2,1,0:T(8,128)(2,1)}, bf16[128,1,32,256]{3,2,1,0:T(8,128)(2,1)}) fusion(bf16[128,2,32,256]{3,2,1,0:T(8,128)(2,1)} %gather_fusion.2), kind=kLoop, calls=%fused_computation.114 | loop fusion | bytes 8388608 | tf_op jit(solution)/shard_map/slice | solution.py:115
  171.3 7.1 %reshape_squeeze.14 = bf16[4096,4,64]{2,1,0:T(4,128)(2,1)} reshape(bf16[128,1,32,256]{3,2,1,0:T(8,128)(2,1)} %get-tuple-element.110) | data formatting | bytes 4194304 | tf_op jit(solution)/shard_map/reshape;squeeze | solution.py:114
  178.4 7.2 %reshape_squeeze.16 = bf16[4096,4,64]{2,1,0:T(4,128)(2,1)} reshape(bf16[128,1,32,256]{3,2,1,0:T(8,128)(2,1)} %get-tuple-element.109) | data formatting | bytes 4194304 | tf_op jit(solution)/shard_map/reshape;squeeze | solution.py:115
  185.6 3.9 %fusion.37 = f32[256,768]{1,0:T(8,128)} fusion(bf16[2048,1792]{1,0:T(8,128)(2,1)} %all-gather.7.cloned.1.call-done, bf16[256,2048]{1,0:T(8,128)(2,1)S(1)} %copy-done.2, f32[2048]{0:T(1024)S(1)} %copy-done.13, f32[2048]{0:T(1024)S(1)} %copy-done.14, f32[256]{0:T(256)S(1)} %add_rsqrt_fusion.1, f32[256]{0:T(256)S(1)} %broadcast_multiply_fusion.1, ...), kind=kOutput, calls=%fused_computation.49 | convolution fusion | flops 808648704 | bytes 5002240 | tf_op jit(solution)/shard_map/dot_general | solution.py:42
  189.5 1.4 copy.80
  191.3 17.7 %maximum_bitcast_fusion = bf16[4,4352,64]{2,0,1:T(4,128)(2,1)S(1)} fusion(bf16[256,4,64]{2,1,0:T(4,128)(2,1)S(1)} %copy.82, bf16[4096,4,64]{2,1,0:T(4,128)(2,1)} %reshape_squeeze.14), kind=kLoop, calls=%fused_computation.20 | loop fusion | flops 1114112 | bytes 4456448 | tf_op jit(solution)/shard_map/transpose | solution.py:124
  208.9 2.7 copy.85
  211.8 17.9 %maximum_bitcast_fusion.1 = bf16[4,4352,64]{2,0,1:T(4,128)(2,1)S(1)} fusion(bf16[256,4,64]{2,1,0:T(4,128)(2,1)S(1)} %copy.83, bf16[4096,4,64]{2,1,0:T(4,128)(2,1)} %reshape_squeeze.16), kind=kLoop, calls=%fused_computation.21 | loop fusion | flops 1114112 | bytes 4456448 | tf_op jit(solution)/shard_map/transpose | solution.py:125
  229.7 2.6 copy.86
  232.4 21.9 %while.11 = (s32[]{:T(128)}, bf16[4,256,64]{1,2,0:T(8,128)(2,1)S(1)}, bf16[4,256,64]{1,2,0:T(8,128)(2,1)S(1)}, bf16[4,4352,64]{2,1,0:T(8,128)(2,1)}, pred[256,43...) while((s32[]{:T(128)}, bf16[4,256,64]{1,2,0:T(8,128)(2,1)S(1)}, ...), condition=%wide.region_10.11_spmd, body=%wide.region_7.10_spmd.sunk | while | flops 294141440 | bytes 16784460 | solution.py:140
  232.4 2.3 fusion.80
  234.7 0.8 fusion.81
  235.5 2.4 fusion.82
  237.8 2.3 fusion.80
  240.2 0.8 fusion.81
  240.9 2.4 fusion.82
  243.3 2.3 fusion.80
  245.7 0.8 fusion.81
  246.4 2.4 fusion.82
  248.8 2.3 fusion.80
  251.1 0.8 fusion.81
  251.9 2.4 fusion.82
  254.3 1.3 slice.115
  255.5 3.4 reshape.322
  258.9 3.5 copy.87
  262.4 1.5 convolution_convert_fusion
  264.0 93.6 %all-gather.9.cloned.1.call-done = bf16[2048,2048]{1,0:T(8,128)(2,1)} async-done(((bf16[256,2048]{1,0:T(8,128)(2,1)}), bf16[2048,2048]{1,0:T(8,128)(2,1)}) %all-gather.9.cloned.1.call-update) | async-done | bytes 8388624 | tf_op jit(solution)/shard_map/all_gather | solution.py:144
  357.6 5.2 %reduce_sum.69 = bf16[256,2048]{1,0:T(8,128)(2,1)S(1)} reduce(bf16[8,256,2048]{2,1,0:T(8,128)(2,1)} %bitcast.76, bf16[]{:T(256)} %constant.191.clone.1), dimensions={0}, to_apply=%region_11.12 | reduce | flops 3670016 | bytes 9437186 | tf_op jit(solution)/shard_map/reduce_sum | solution.py:144
  362.8 1.9 convert_reduce_fusion.1
  365.7 3.0 fusion.43
  368.9 0.9 copy.89
  369.8 1.6 constant_dynamic-slice_fusion
  (93 shorter events, 7.6 us)
Async XLA Ops:
  7.2 34.9 %copy-start = (bf16[48,2,32,256]{3,2,1,0:T(8,128)(2,1)S(1)}, bf16[48,2,32,256]{3,2,1,0:T(8,128)(2,1)}, u32[]{:S(2)}) copy-start(bf16[48,2,32,256]{3,2,1,0:T(8,128)(2,1)} %param.26) | copy-start | bytes 4718596
  7.2 51.6 %all-gather.5.cloned.1.call-start = ((), (), s32[]{:S(2)}) async-start(), calls=%async_computation.2 | async-start | bytes 1179648 | tf_op jit(solution)/shard_map/all_gather | solution.py:65
  7.9 177.7 %all-gather.7.cloned.1.call-start = ((), (), s32[]{:S(2)}) async-start(), calls=%async_computation.3 | async-start | bytes 7454720 | tf_op jit(solution)/shard_map/all_gather | solution.py:76
  44.9 6.0 %copy-start.8 = (f32[3,256]{1,0:T(4,128)S(1)}, f32[3,256]{1,0:T(4,128)}, u32[]{:S(2)}) copy-start(f32[3,256]{1,0:T(4,128)} %param.25) | copy-start | bytes 9220
  44.9 6.0 %copy-start.5 = (s32[256]{0:T(256)S(1)}, s32[256]{0:T(256)}, u32[]{:S(2)}) copy-start(s32[256]{0:T(256)} %param.33) | copy-start | bytes 3076
  44.9 9.3 %copy-start.6 = (s32[4]{0:T(128)S(1)}, s32[4]{0:T(128)}, u32[]{:S(2)}) copy-start(s32[4]{0:T(128)} %param.34) | copy-start | bytes 52
  44.9 10.2 %copy-start.10 = (pred[4096]{0:T(1024)(128)(4,1)S(1)}, pred[4096]{0:T(1024)(128)(4,1)}, u32[]{:S(2)}) copy-start(pred[4096]{0:T(1024)(128)(4,1)} %constant.224) | copy-start | bytes 12292
  44.9 10.2 %copy-start.11 = (pred[4096]{0:T(1024)(128)(4,1)S(1)}, pred[4096]{0:T(1024)(128)(4,1)}, u32[]{:S(2)}) copy-start(pred[4096]{0:T(1024)(128)(4,1)} %constant.225) | copy-start | bytes 12292
  44.9 10.2 %copy-start.12 = (pred[4096]{0:T(1024)(128)(4,1)S(1)}, pred[4096]{0:T(1024)(128)(4,1)}, u32[]{:S(2)}) copy-start(pred[4096]{0:T(1024)(128)(4,1)} %constant.226) | copy-start | bytes 12292
  44.9 116.7 %all-to-all-start.1 = ((bf16[64,2,2,32,256]{4,3,2,1,0:T(8,128)(2,1)}), bf16[64,2,2,32,256]{4,3,2,1,0:T(8,128)(2,1)}, u32[]{:S(2)}, u32[]{:S(2)}) async-start(bf16[64,2,2,32,256]{4,3,2,1,0:T(8,128)(2,1)} %bitcast.75), calls=%async_computation.1 | async-start | bytes 8388608 | tf_op jit(solution)/shard_map/all_to_all | solution.py:110
  50.8 306.8 %all-gather.9.cloned.1.call-start = ((), (), s32[]{:S(2)}) async-start(), calls=%async_computation.4 | async-start | bytes 9437184 | tf_op jit(solution)/shard_map/all_gather | solution.py:144
  178.4 7.2 %copy-start.2 = (bf16[256,2048]{1,0:T(8,128)(2,1)S(1)}, bf16[256,2048]{1,0:T(8,128)(2,1)}, u32[]{:S(2)}) copy-start(bf16[256,2048]{1,0:T(8,128)(2,1)} %all-gather.5.cloned.1.call-done) | copy-start | bytes 3145732
  178.4 7.2 %copy-start.13 = (f32[2048]{0:T(1024)S(1)}, f32[2048]{0:T(1024)}, u32[]{:S(2)}) copy-start(f32[2048]{0:T(1024)} %param.23) | copy-start | bytes 24580
  178.4 7.2 %copy-start.14 = (f32[2048]{0:T(1024)S(1)}, f32[2048]{0:T(1024)}, u32[]{:S(2)}) copy-start(f32[2048]{0:T(1024)} %param.22) | copy-start | bytes 24580
  229.7 2.7 copy-start.4
  258.9 5.0 %copy-start.9 = (f32[3,256]{1,0:T(4,128)S(1)}, f32[3,256]{1,0:T(4,128)}, u32[]{:S(2)}) copy-start(f32[3,256]{1,0:T(4,128)} %param.32) | copy-start | bytes 9220
  357.6 5.2 %copy-start.7 = (f32[2048]{0:T(1024)S(1)}, f32[2048]{0:T(1024)}, u32[]{:S(2)}) copy-start(f32[2048]{0:T(1024)} %param.28) | copy-start | bytes 24580
  362.8 2.9 copy-start.15
  362.8 2.9 copy-start.16
  364.7 1.0 copy-start.3
  365.1 6.3 %copy-start.1 = (bf16[48,2,32,256]{3,2,1,0:T(8,128)(2,1)S(1)}, bf16[48,2,32,256]{3,2,1,0:T(8,128)(2,1)}, u32[]{:S(2)}) copy-start(bf16[48,2,32,256]{3,2,1,0:T(8,128)(2,1)} %param.26) | copy-start | bytes 4718596
Sparse Core Ops, SparseCore 0:
  10.0 43.6 all-gather.4
  57.6 113.7 all-gather.6
  264.1 93.4 all-gather.8
